TPU v7x, 32 devices: a whole 2x2x4 slice. The times are simulated.
32 devices in a mesh: ctx: 8 (over z, y), tp: 4 (over x, core).
Axes of the slice: x: 2, y: 2, z: 4, core: 2. Of those that a mesh axis runs over, the one named last changes fastest.
Arguments:
- tokens: bfloat16 [1024, 4096], P('ctx'), may hold values from -6 to 6
- w_query: bfloat16 [4096, 2048], P('ctx', 'tp'), may hold values from -0.09375 to 0.09375
- w_key: bfloat16 [4096, 2048], P('ctx', 'tp'), may hold values from -0.09375 to 0.09375
- w_value: bfloat16 [4096, 2048], P('ctx', 'tp'), may hold values from -0.09375 to 0.09375
- taps_query: float32 [3, 2048], P(None, 'tp'), may hold values from -3.5 to 3.5
- taps_key: float32 [3, 2048], P(None, 'tp'), may hold values from -3.5 to 3.5
- taps_value: float32 [3, 2048], P(None, 'tp'), may hold values from -3.5 to 3.5
- decay_rate: float32 [16, 2048], P(None, 'tp'), may hold values from 1e-05 to 0.03
- residue: float32 [16, 2048], P(None, 'tp'), may hold values from -1.5 to 1.5
- skip_gain: float32 [2048], P('tp'), may hold values from -3 to 3
- w_out: bfloat16 [2048, 4096], P('ctx', 'tp'), may hold values from -0.125 to 0.125
Outputs:
- layer_out: bfloat16 [1024, 4096], P('ctx', 'tp')
All inputs are finite; a program needn't handle non-finite values.
Results may differ from a plain program's by a relative error of at most 0.015.
Values may be sent and summed in bfloat16 or wider, within the bound.
No kernel may reach another device: no remote copies, remote signals or barrier semaphores. Data moves between devices by JAX's collectives and lax.ppermute only.
A program may use at most 128 MiB of HBM per device.

v0:
```python
import math
import jax
import jax.numpy as jnp
from jax import lax
from jax.sharding import PartitionSpec as P


def exact_mul(left, right):
    return jnp.matmul(left, right, precision=lax.Precision.HIGHEST)


def dft_tables(count):
    index = jnp.arange(count, dtype=jnp.int32)
    angle = (index[:, None] * index[None, :] % count).astype(jnp.float32) * (2.0 * math.pi / count)
    return (jnp.cos(angle), jnp.sin(angle))


def long_conv(signal, rates, residues, skips, rows_a, cols_b):
    half = rows_a // 2
    total_len = rows_a * cols_b
    length = half * cols_b
    cos_a, sin_a = dft_tables(rows_a)
    cos_b, sin_b = dft_tables(cols_b)
    index_a = jnp.arange(rows_a, dtype=jnp.int32)
    index_b = jnp.arange(cols_b, dtype=jnp.int32)
    twist = (index_a[:, None] * index_b[None, :] % total_len).astype(jnp.float32) * (
        2.0 * math.pi / total_len
    )
    twist_cos = jnp.cos(twist)
    twist_sin = jnp.sin(twist)
    times = jnp.arange(length, dtype=jnp.float32)

    def one_channel(items):
        channel, rate, weight, skip = items
        channel_f = channel.astype(jnp.float32)
        coefs = weight * jnp.sqrt(2.0 * rate)
        kernel = jnp.sum(coefs[:, None] * jnp.exp(-rate[:, None] * times[None, :]), axis=0)
        stacked = jnp.stack([channel_f, kernel]).reshape(2, half, cols_b)
        first_re = exact_mul(cos_a[:, :half], stacked)
        first_im = -exact_mul(sin_a[:, :half], stacked)
        turned_re = first_re * twist_cos + first_im * twist_sin
        turned_im = first_im * twist_cos - first_re * twist_sin
        spec_re = exact_mul(turned_re, cos_b) + exact_mul(turned_im, sin_b)
        spec_im = exact_mul(turned_im, cos_b) - exact_mul(turned_re, sin_b)
        prod_re = spec_re[0] * spec_re[1] - spec_im[0] * spec_im[1]
        prod_im = spec_re[0] * spec_im[1] + spec_im[0] * spec_re[1]
        back_re = exact_mul(prod_re, cos_b) - exact_mul(prod_im, sin_b)
        back_im = exact_mul(prod_im, cos_b) + exact_mul(prod_re, sin_b)
        unturned_re = back_re * twist_cos - back_im * twist_sin
        unturned_im = back_im * twist_cos + back_re * twist_sin
        result = (
            exact_mul(cos_a[:half], unturned_re) - exact_mul(sin_a[:half], unturned_im)
        ) / total_len
        return result.reshape(length) + skip * channel_f

    return lax.map(one_channel, (signal, rates, residues, skips))


def body(
    tokens,
    w_query,
    w_key,
    w_value,
    taps_query,
    taps_key,
    taps_value,
    decay_rate,
    residue,
    skip_gain,
    w_out,
):
    tok_count = tokens.shape[0]
    width_part = w_query.shape[1]

    def add_rows(piece):
        return jnp.dot(tokens, piece, preferred_element_type=jnp.float32)

    queries = add_rows(lax.all_gather(w_query, "ctx", axis=0, tiled=True))
    keys_proj = add_rows(lax.all_gather(w_key, "ctx", axis=0, tiled=True))
    values_proj = add_rows(lax.all_gather(w_value, "ctx", axis=0, tiled=True))
    queries = queries.astype(jnp.bfloat16)
    keys_proj = keys_proj.astype(jnp.bfloat16)
    values_proj = values_proj.astype(jnp.bfloat16)
    ctx_count = lax.axis_size("ctx")
    chan_count = width_part // ctx_count
    first = lax.axis_index("ctx") * chan_count
    rates = lax.dynamic_slice_in_dim(decay_rate, first, chan_count, 1).T
    residues = lax.dynamic_slice_in_dim(residue, first, chan_count, 1).T
    skips = lax.dynamic_slice_in_dim(skip_gain, first, chan_count, 0)
    query_chan, key_chan, value_chan = (
        lax.all_to_all(queries.T, "ctx", split_axis=0, concat_axis=1, tiled=True),
        lax.all_to_all(keys_proj.T, "ctx", split_axis=0, concat_axis=1, tiled=True),
        lax.all_to_all(values_proj.T, "ctx", split_axis=0, concat_axis=1, tiled=True),
    )

    def conv_channels(signal_in, taps):
        taps_part = lax.dynamic_slice_in_dim(taps, first, chan_count, 1)
        padded = jnp.pad(signal_in.astype(jnp.float32), ((0, 0), (2, 0)))
        return (
            taps_part[0][:, None] * padded[:, 2:]
            + taps_part[1][:, None] * padded[:, 1:-1]
            + taps_part[2][:, None] * padded[:, :-2]
        )

    gate_channels = conv_channels(query_chan, taps_query).astype(jnp.bfloat16)
    signal = (conv_channels(key_chan, taps_key) * conv_channels(value_chan, taps_value)).astype(
        jnp.bfloat16
    )
    mixed_long = long_conv(signal, rates, residues, skips, tok_count, 2 * ctx_count).astype(
        jnp.bfloat16
    )
    outgoing = (gate_channels.astype(jnp.float32) * mixed_long.astype(jnp.float32)).astype(
        jnp.bfloat16
    )
    gated = lax.all_to_all(outgoing, "ctx", split_axis=1, concat_axis=0, tiled=True).T
    features = lax.all_gather(gated, "tp", axis=1, tiled=True)
    result = jnp.dot(
        features,
        lax.all_gather(w_out, "ctx", axis=0, tiled=True),
        preferred_element_type=jnp.float32,
    )
    return result.astype(jnp.bfloat16)


def solution(mesh):
    in_specs = (
        P("ctx", None),
        P("ctx", "tp"),
        P("ctx", "tp"),
        P("ctx", "tp"),
        P(None, "tp"),
        P(None, "tp"),
        P(None, "tp"),
        P(None, "tp"),
        P(None, "tp"),
        P("tp"),
        P("ctx", "tp"),
    )
    out_specs = P("ctx", "tp")
    return jax.shard_map(body, mesh=mesh, in_specs=in_specs, out_specs=out_specs, check_vma=False)
```

profile of v0, /device:TPU:0, one launch (start us, length us, event | category | flops | bytes accessed | tf_op | source)
XLA Modules:
  0.0 559.2 jit_solution(9386341728542071466)
XLA Ops:
  6.5 0.7 all-gather.9.cloned.1.call-update
  7.3 0.7 all-gather.7.cloned.1.call-update
  8.1 0.7 all-gather.5.cloned.1.call-update
  9.6 0.8 constant_dynamic-slice_fusion.4
  10.4 0.8 constant_dynamic-slice_fusion.2
  11.4 0.8 dynamic_slice.38
  12.1 0.8 constant_dynamic-slice_fusion.6
  12.9 72.7 %all-gather.9.cloned.1.call-done = bf16[4096,512]{1,0:T(8,128)(2,1)} async-done(((bf16[512,512]{1,0:T(8,128)(2,1)}), bf16[4096,512]{1,0:T(8,128)(2,1)}) %all-gather.9.cloned.1.call-update) | async-done | bytes 4194320 | tf_op jit(solution)/shard_map/all_gather | solution.py:80
  85.6 4.1 convolution_convert_fusion.1
  89.8 3.4 all-to-all-start.2
  93.1 67.3 %all-gather.7.cloned.1.call-done = bf16[4096,512]{1,0:T(8,128)(2,1)} async-done(((bf16[512,512]{1,0:T(8,128)(2,1)}), bf16[4096,512]{1,0:T(8,128)(2,1)}) %all-gather.7.cloned.1.call-update) | async-done | bytes 4194320 | tf_op jit(solution)/shard_map/all_gather | solution.py:79
  160.5 4.1 convolution_convert_fusion.2
  164.6 69.7 %all-gather.5.cloned.1.call-done = bf16[4096,512]{1,0:T(8,128)(2,1)} async-done(((bf16[512,512]{1,0:T(8,128)(2,1)}), bf16[4096,512]{1,0:T(8,128)(2,1)}) %all-gather.5.cloned.1.call-update) | async-done | bytes 4194320 | tf_op jit(solution)/shard_map/all_gather | solution.py:78
  234.3 4.1 convolution_convert_fusion.3
  238.4 3.4 all-to-all-start.1
  241.8 9.0 %all-to-all-done.1 = bf16[8,64,128]{2,1,0:T(8,128)(2,1)S(1)} async-done(((bf16[8,64,128]{2,1,0:T(8,128)(2,1)}), bf16[8,64,128]{2,1,0:T(8,128)(2,1)S(1)}, u32[]{:S(2)}, u32[]{:S(2)}) %all-to-all-start.1) | async-done | bytes 131104 | tf_op jit(solution)/shard_map/all_to_all | solution.py:92
  250.9 4.1 all-to-all-start
  255.4 273.1 %while.12 = (s32[]{:T(128)}, bf16[64,1024]{1,0:T(8,128)(2,1)S(1)}, bf16[64,1024]{1,0:T(8,128)(2,1)S(1)}, f32[64,16]{1,0:T(8,128)S(1)}, f32[64,16]{1,0:T(8,128)S(...) while((s32[]{:T(128)}, bf16[64,1024]{1,0:T(8,128)(2,1)S(1)}, ...), condition=%wide.region_2.3_spmd.clone.clone, body=%wide.region_0.2_spmd.clone.clone.sunk | while | flops 14420018 | bytes 821765 | solution.py:56
  262.7 0.6 dynamic_slice.73
  275.5 0.6 dynamic_slice.73
  288.3 0.6 dynamic_slice.73
  528.8 13.1 %all_to_all.58 = bf16[64,8,128]{2,0,1:T(8,128)(2,1)S(1)} all-to-all(bf16[64,8,128]{2,0,1:T(8,128)(2,1)S(1)} %copy_bitcast_fusion.3), channel_id=1, replica_groups=mesh['ctx'=8,'tp'=4] {'ctx'}, dimensions={1} | all-to-all | bytes 262144 | tf_op jit(solution)/shard_map/all_to_all | solution.py:115
  541.9 7.1 %all_gather.18 = bf16[128,2048]{0,1:T(8,128)(2,1)S(1)} all-gather(bf16[128,512]{0,1:T(8,128)(2,1)S(1)} %bitcast.126), channel_id=1, replica_groups=mesh['ctx'=8,'tp'=4] {'tp'}, dimensions={1}, use_global_device_ids=true | all-gather | bytes 655360 | tf_op jit(solution)/shard_map/all_gather | solution.py:116
  549.1 3.6 convolution_convert_fusion
  (1683 shorter events, 265.6 us)
Async XLA Ops:
  6.5 79.1 %copy-start = (bf16[128,4096]{1,0:T(8,128)(2,1)S(1)}, bf16[128,4096]{1,0:T(8,128)(2,1)}, u32[]{:S(2)}) copy-start(bf16[128,4096]{1,0:T(8,128)(2,1)} %param.13) | copy-start | bytes 3145732
  6.5 79.1 %all-gather.9.cloned.1.call-start = ((), (), s32[]{:S(2)}) async-start(), calls=%async_computation.6 | async-start | bytes 4718592 | tf_op jit(solution)/shard_map/all_gather | solution.py:80
  7.3 153.2 %all-gather.7.cloned.1.call-start = ((), (), s32[]{:S(2)}) async-start(), calls=%async_computation.5 | async-start | bytes 4718592 | tf_op jit(solution)/shard_map/all_gather | solution.py:79
  8.0 226.3 %all-gather.5.cloned.1.call-start = ((), (), s32[]{:S(2)}) async-start(), calls=%async_computation.4 | async-start | bytes 4718592 | tf_op jit(solution)/shard_map/all_gather | solution.py:78
  8.7 540.3 %all-gather.11.cloned.1.call-start = ((), (), s32[]{:S(2)}) async-start(), calls=%async_computation.7 | async-start | bytes 4718592 | tf_op jit(solution)/shard_map/all_gather | solution.py:119
  89.8 148.7 %all-to-all-start.2 = ((bf16[8,64,128]{2,1,0:T(8,128)(2,1)}), bf16[8,64,128]{2,1,0:T(8,128)(2,1)S(1)}, u32[]{:S(2)}, u32[]{:S(2)}) async-start(bf16[8,64,128]{2,1,0:T(8,128)(2,1)} %bitcast.11), calls=%async_computation.2 | async-start | bytes 262144 | tf_op jit(solution)/shard_map/all_to_all | solution.py:93
  238.4 12.4 %all-to-all-start.1 = ((bf16[8,64,128]{2,1,0:T(8,128)(2,1)}), bf16[8,64,128]{2,1,0:T(8,128)(2,1)S(1)}, u32[]{:S(2)}, u32[]{:S(2)}) async-start(bf16[8,64,128]{2,1,0:T(8,128)(2,1)} %bitcast.6), calls=%async_computation.1 | async-start | bytes 262144 | tf_op jit(solution)/shard_map/all_to_all | solution.py:92
  250.9 277.6 %all-to-all-start = ((bf16[8,64,128]{2,1,0:T(8,128)(2,1)}), bf16[8,64,128]{2,1,0:T(8,128)(2,1)S(1)}, u32[]{:S(2)}, u32[]{:S(2)}) async-start(bf16[8,64,128]{2,1,0:T(8,128)(2,1)} %bitcast.1), calls=%async_computation | async-start | bytes 262144 | tf_op jit(solution)/shard_map/all_to_all | solution.py:91
Sparse Core Ops, SparseCore 0:
  9.5 76.0 all-gather.8
  87.7 72.6 all-gather.6
  162.6 71.6 all-gather.4
  236.3 75.7 all-gather.10
where the time goes:
time: 561 us; the launch traced here: 559 us
  waiting for transfers between devices  221 us (39%)
  matrix products  160 us (29%)
  local copies, waits for them, and re-layouts  74.8 us (13%)
  other arithmetic  51.3 us (9%)
  blocking collectives  20.3 us (4%)
  between operations  13.2 us (2%)
  starting transfers between devices  11 us (2%)
  loops' own time  7.56 us (1%)
    dot_general x768, matrix products, exact_mul(): return jnp.matmul(left, right, precision=lax.Precision.HIGHEST)  144 us
    all_gather x1, waiting for transfers between devices, body(): values_proj = add_rows(lax.all_gather(w_value, 'ctx', axis=0, tiled=True))  72.7 us
    all_gather x1, waiting for transfers between devices, body(): queries = add_rows(lax.all_gather(w_query, 'ctx', axis=0, tiled=True))  69.7 us
    all_gather x1, waiting for transfers between devices, body(): keys_proj = add_rows(lax.all_gather(w_key, 'ctx', axis=0, tiled=True))  67.3 us
    dynamic_slice x64, local copies, waits for them, and re-layouts, long_conv(): return lax.map(one_channel, (signal, rates, residues, skips))  37.7 us
    add x64, other arithmetic, one_channel(): return result.reshape(length) + skip * channel_f  36.7 us
    another operation x256, local copies, waits for them, and re-layouts, one_channel(): stacked = jnp.stack([channel_f, kernel]).reshape(2, half, cols_b)  17.5 us
    all_to_all x1, blocking collectives, body(): lax.all_to_all(outgoing, 'ctx', split_axis=1, concat_axis=0, tiled=True)  13.1 us
  transfers between devices with their start and end apart: 7, of which 4 were waited for; matrix products, arithmetic and copies ran while one was open for 50% of the time, Pallas kernels for 0%

commit v1 on v0

--- a/solution.py
+++ b/solution.py
@@ -3,6 +3,25 @@
 import jax.numpy as jnp
 from jax import lax
 from jax.sharding import PartitionSpec as P
+
+
+def collect(x, axis, dim):
+    size, index, rows = (lax.axis_size(axis), lax.axis_index(axis), x.shape[dim])
+    right = [(i, (i + 1) % size) for i in range(size)]
+    left = [(i, (i - 1) % size) for i in range(size)]
+    out = jnp.zeros((*x.shape[:dim], size * rows, *x.shape[dim + 1 :]), x.dtype)
+    out = lax.dynamic_update_slice_in_dim(out, x, index * rows, axis=dim)
+    from_left = from_right = x
+    middle = size // 2
+    for lap in range(1, middle + 1):
+        from_left = lax.ppermute(from_left, axis, right)
+        out = lax.dynamic_update_slice_in_dim(out, from_left, (index - lap) % size * rows, axis=dim)
+        if lap < size - middle:
+            from_right = lax.ppermute(from_right, axis, left)
+            out = lax.dynamic_update_slice_in_dim(
+                out, from_right, (index + lap) % size * rows, axis=dim
+            )
+    return out
 
 
 def exact_mul(left, right):
@@ -75,7 +94,7 @@
     def add_rows(piece):
         return jnp.dot(tokens, piece, preferred_element_type=jnp.float32)
 
-    queries = add_rows(lax.all_gather(w_query, "ctx", axis=0, tiled=True))
+    queries = add_rows(collect(w_query, "ctx", 0))
     keys_proj = add_rows(lax.all_gather(w_key, "ctx", axis=0, tiled=True))
     values_proj = add_rows(lax.all_gather(w_value, "ctx", axis=0, tiled=True))
     queries = queries.astype(jnp.bfloat16)

time: 561 us -> 542 us (0.966)
  waiting for transfers between devices: 221 us -> 176 us
  starting transfers between devices: 11 us -> 32.3 us
    ppermute x0 -> x7, waiting for transfers between devices: none -> 89.9 us  [the longest x4 87 us: collect(): from_left = lax.ppermute(from_left, axis, right)]
    all_gather x1, waiting for transfers between devices: 72.7 us -> 1.01 us  [body(): values_proj = add_rows(lax.all_gather(w_value, 'ctx', axis=0, tiled=True))]
    all_gather x1 -> x0, waiting for transfers between devices: 69.7 us -> none  [body(): queries = add_rows(lax.all_gather(w_query, 'ctx', axis=0, tiled=True))]
    ppermute x0 -> x7, starting transfers between devices: none -> 19 us  [the longest x4 11 us: collect(): from_left = lax.ppermute(from_left, axis, right)]
    all_to_all x1, waiting for transfers between devices: 0.01 us -> 7.66 us  [body(): lax.all_to_all(queries.T, 'ctx', split_axis=0, concat_axis=1, tiled=True)]
  transfers between devices with their start and end apart: 7 -> 13, of which waited for: 4 -> 10; matrix products, arithmetic and copies ran while one was open for 50% -> 53% of each run, Pallas kernels for 0% -> 0%
where the time goes in v1:
time: 542 us; the launch traced here: 540 us
  waiting for transfers between devices  176 us (32%)
  matrix products  158 us (29%)
  local copies, waits for them, and re-layouts  77.7 us (14%)
  other arithmetic  56.8 us (10%)
  starting transfers between devices  32.3 us (6%)
  blocking collectives  19 us (4%)
  between operations  13.2 us (2%)
  loops' own time  7.6 us (1%)
    dot_general x768, matrix products, exact_mul(): return jnp.matmul(left, right, precision=lax.Precision.HIGHEST)  144 us
    ppermute x4, waiting for transfers between devices, collect(): from_left = lax.ppermute(from_left, axis, right)  87 us
    all_gather x1, waiting for transfers between devices, body(): keys_proj = add_rows(lax.all_gather(w_key, 'ctx', axis=0, tiled=True))  67.5 us
    add x64, other arithmetic, one_channel(): return result.reshape(length) + skip * channel_f  42.2 us
    dynamic_slice x64, local copies, waits for them, and re-layouts, long_conv(): return lax.map(one_channel, (signal, rates, residues, skips))  38 us
    another operation x256, local copies, waits for them, and re-layouts, one_channel(): stacked = jnp.stack([channel_f, kernel]).reshape(2, half, cols_b)  17.5 us
    all_to_all x1, blocking collectives, body(): lax.all_to_all(outgoing, 'ctx', split_axis=1, concat_axis=0, tiled=True)  11.9 us
    ppermute x4, starting transfers between devices, collect(): from_left = lax.ppermute(from_left, axis, right)  11 us
  transfers between devices with their start and end apart: 13, of which 10 were waited for; matrix products, arithmetic and copies ran while one was open for 53% of the time, Pallas kernels for 0%

profile of v1, /device:TPU:0, one launch (start us, length us, event | category | flops | bytes accessed | tf_op | source)
XLA Modules:
  0.0 540.3 jit_solution(811241277233286650)
XLA Ops:
  8.1 3.0 collective-permute-start
  11.1 3.1 collective-permute-start.1
  14.2 25.2 %collective-permute-done = bf16[512,512]{1,0:T(8,128)(2,1)S(1)} collective-permute-done((bf16[512,512]{1,0:T(8,128)(2,1)}, bf16[512,512]{1,0:T(8,128)(2,1)S(1)}, u32[]{:S(2)}, u32[]{:S(2)}) %collective-permute-start) | collective-permute-done | bytes 524320 | tf_op jit(solution)/shard_map/ppermute | solution.py:17
  39.4 2.4 collective-permute-start.2
  42.6 3.1 collective-permute-start.3
  46.0 23.9 %collective-permute-done.2 = bf16[512,512]{1,0:T(8,128)(2,1)S(1)} collective-permute-done((bf16[512,512]{1,0:T(8,128)(2,1)S(1)}, bf16[512,512]{1,0:T(8,128)(2,1)S(1)}, u32[]{:S(2)}, u32[]{:S(2)}) %collective-permute-start.2) | collective-permute-done | bytes 524320 | tf_op jit(solution)/shard_map/ppermute | solution.py:17
  69.9 3.0 collective-permute-start.4
  75.4 1.9 collective-permute-start.5
  77.3 28.6 %collective-permute-done.4 = bf16[512,512]{1,0:T(8,128)(2,1)} collective-permute-done((bf16[512,512]{1,0:T(8,128)(2,1)S(1)}, bf16[512,512]{1,0:T(8,128)(2,1)}, u32[]{:S(2)}, u32[]{:S(2)}) %collective-permute-start.4) | collective-permute-done | bytes 524320 | tf_op jit(solution)/shard_map/ppermute | solution.py:17
  105.9 2.6 collective-permute-start.6
  112.3 9.3 %collective-permute-done.6 = bf16[512,512]{1,0:T(8,128)(2,1)S(1)} collective-permute-done((bf16[512,512]{1,0:T(8,128)(2,1)}, bf16[512,512]{1,0:T(8,128)(2,1)S(1)}, u32[]{:S(2)}, u32[]{:S(2)}) %collective-permute-start.6) | collective-permute-done | bytes 524320 | tf_op jit(solution)/shard_map/ppermute | solution.py:17
  121.6 2.0 convolution_convert_fusion.3
  123.6 6.4 %all-to-all-start = ((bf16[8,64,128]{2,1,0:T(8,128)(2,1)}), bf16[8,64,128]{2,1,0:T(8,128)(2,1)S(1)}, u32[]{:S(2)}, u32[]{:S(2)}) async-start(bf16[8,64,128]{2,1,0:T(8,128)(2,1)} %bitcast.1), calls=%async_computation | async-start | bytes 262144 | tf_op jit(solution)/shard_map/all_to_all | solution.py:110
  131.7 7.7 %all-to-all-done = bf16[8,64,128]{2,1,0:T(8,128)(2,1)S(1)} async-done(((bf16[8,64,128]{2,1,0:T(8,128)(2,1)}), bf16[8,64,128]{2,1,0:T(8,128)(2,1)S(1)}, u32[]{:S(2)}, u32[]{:S(2)}) %all-to-all-start) | async-done | bytes 131104 | tf_op jit(solution)/shard_map/all_to_all | solution.py:110
  140.4 4.1 convolution_convert_fusion.1
  144.6 3.4 all-to-all-start.2
  148.0 67.5 %all-gather.4.cloned.1.call-done = bf16[4096,512]{1,0:T(8,128)(2,1)} async-done(((bf16[512,512]{1,0:T(8,128)(2,1)}), bf16[4096,512]{1,0:T(8,128)(2,1)}) %all-gather.4.cloned.1.call-update) | async-done | bytes 4194320 | tf_op jit(solution)/shard_map/all_gather | solution.py:98
  215.5 4.1 convolution_convert_fusion.2
  219.6 3.4 all-to-all-start.1
  223.0 8.3 %all-to-all-done.1 = bf16[8,64,128]{2,1,0:T(8,128)(2,1)S(1)} async-done(((bf16[8,64,128]{2,1,0:T(8,128)(2,1)}), bf16[8,64,128]{2,1,0:T(8,128)(2,1)S(1)}, u32[]{:S(2)}, u32[]{:S(2)}) %all-to-all-start.1) | async-done | bytes 131104 | tf_op jit(solution)/shard_map/all_to_all | solution.py:111
  231.8 279.0 %while.12 = (s32[]{:T(128)}, bf16[64,1024]{1,0:T(8,128)(2,1)S(1)}, bf16[64,1024]{1,0:T(8,128)(2,1)S(1)}, f32[64,16]{1,0:T(8,128)S(1)}, f32[64,16]{1,0:T(8,128)S(...) while((s32[]{:T(128)}, bf16[64,1024]{1,0:T(8,128)(2,1)S(1)}, ...), condition=%wide.region_2.3_spmd.clone.clone, body=%wide.region_0.2_spmd.clone.clone.sunk | while | flops 14420018 | bytes 821765 | solution.py:75
  511.1 11.9 %all_to_all.58 = bf16[64,8,128]{2,0,1:T(8,128)(2,1)S(1)} all-to-all(bf16[64,8,128]{2,0,1:T(8,128)(2,1)S(1)} %copy_bitcast_fusion.3), channel_id=1, replica_groups=mesh['ctx'=8,'tp'=4] {'ctx'}, dimensions={1} | all-to-all | bytes 262144 | tf_op jit(solution)/shard_map/all_to_all | solution.py:134
  523.0 7.1 %all_gather.14 = bf16[128,2048]{0,1:T(8,128)(2,1)S(1)} all-gather(bf16[128,512]{0,1:T(8,128)(2,1)S(1)} %bitcast.126), channel_id=1, replica_groups=mesh['ctx'=8,'tp'=4] {'tp'}, dimensions={1}, use_global_device_ids=true | all-gather | bytes 655360 | tf_op jit(solution)/shard_map/all_gather | solution.py:135
  530.2 3.6 convolution_convert_fusion
  (1705 shorter events, 283.8 us)
Async XLA Ops:
  6.5 115.1 %copy-start = (bf16[128,4096]{1,0:T(8,128)(2,1)S(1)}, bf16[128,4096]{1,0:T(8,128)(2,1)}, u32[]{:S(2)}) copy-start(bf16[128,4096]{1,0:T(8,128)(2,1)} %param.13) | copy-start | bytes 3145732
  6.5 67.4 %copy-start.1 = (bf16[512,512]{1,0:T(8,128)(2,1)S(1)}, bf16[512,512]{1,0:T(8,128)(2,1)}, u32[]{:S(2)}) copy-start(bf16[512,512]{1,0:T(8,128)(2,1)} %param.14) | copy-start | bytes 1572868
  6.5 133.9 %all-gather.6.cloned.1.call-start = ((), (), s32[]{:S(2)}) async-start(), calls=%async_computation.5 | async-start | bytes 4718592 | tf_op jit(solution)/shard_map/all_gather | solution.py:99
  7.3 208.2 %all-gather.4.cloned.1.call-start = ((), (), s32[]{:S(2)}) async-start(), calls=%async_computation.4 | async-start | bytes 4718592 | tf_op jit(solution)/shard_map/all_gather | solution.py:98
  8.0 522.1 %all-gather.8.cloned.1.call-start = ((), (), s32[]{:S(2)}) async-start(), calls=%async_computation.6 | async-start | bytes 4718592 | tf_op jit(solution)/shard_map/all_gather | solution.py:138
  8.1 31.4 %collective-permute-start = (bf16[512,512]{1,0:T(8,128)(2,1)}, bf16[512,512]{1,0:T(8,128)(2,1)S(1)}, u32[]{:S(2)}, u32[]{:S(2)}) collective-permute-start(bf16[512,512]{1,0:T(8,128)(2,1)} %param.14), channel_id=1, source_target_pairs={{0,4},{4,8},{8,12},{12,16},{16,20},{20,24},{24,28},{28,0},{1,5},{5... | collective-permute-start | bytes 1572872 | tf_op jit(solution)/shard_map/ppermute | solution.py:17
  11.1 31.5 %collective-permute-start.1 = (bf16[512,512]{1,0:T(8,128)(2,1)}, bf16[512,512]{1,0:T(8,128)(2,1)S(1)}, u32[]{:S(2)}, u32[]{:S(2)}) collective-permute-start(bf16[512,512]{1,0:T(8,128)(2,1)} %param.14), channel_id=1, source_target_pairs={{0,28},{4,0},{8,4},{12,8},{16,12},{20,16},{24,20},{28,24},{1,29},{... | collective-permute-start | bytes 1572872 | tf_op jit(solution)/shard_map/ppermute | solution.py:20
  39.4 30.5 %collective-permute-start.2 = (bf16[512,512]{1,0:T(8,128)(2,1)S(1)}, bf16[512,512]{1,0:T(8,128)(2,1)S(1)}, u32[]{:S(2)}, u32[]{:S(2)}) collective-permute-start(bf16[512,512]{1,0:T(8,128)(2,1)S(1)} %collective-permute-done), channel_id=1, source_target_pairs={{0,4},{4,8},{8,12},{12,16},{16,20},{20,24},{24,28},{28,0},{1,5},{5... | collective-permute-start | bytes 1572872 | tf_op jit(solution)/shard_map/ppermute | solution.py:17
  42.6 32.8 %collective-permute-start.3 = (bf16[512,512]{1,0:T(8,128)(2,1)S(1)}, bf16[512,512]{1,0:T(8,128)(2,1)}, u32[]{:S(2)}, u32[]{:S(2)}) collective-permute-start(bf16[512,512]{1,0:T(8,128)(2,1)S(1)} %collective-permute-done.1), channel_id=1, source_target_pairs={{0,28},{4,0},{8,4},{12,8},{16,12},{20,16},{24,20},{28,24},{1,29},{... | collective-permute-start | bytes 1572872 | tf_op jit(solution)/shard_map/ppermute | solution.py:20
  69.9 36.0 %collective-permute-start.4 = (bf16[512,512]{1,0:T(8,128)(2,1)S(1)}, bf16[512,512]{1,0:T(8,128)(2,1)}, u32[]{:S(2)}, u32[]{:S(2)}) collective-permute-start(bf16[512,512]{1,0:T(8,128)(2,1)S(1)} %collective-permute-done.2), channel_id=1, source_target_pairs={{0,4},{4,8},{8,12},{12,16},{16,20},{20,24},{24,28},{28,0},{1,5},{5... | collective-permute-start | bytes 1572872 | tf_op jit(solution)/shard_map/ppermute | solution.py:17
  75.4 36.8 %collective-permute-start.5 = (bf16[512,512]{1,0:T(8,128)(2,1)}, bf16[512,512]{1,0:T(8,128)(2,1)S(1)}, u32[]{:S(2)}, u32[]{:S(2)}) collective-permute-start(bf16[512,512]{1,0:T(8,128)(2,1)} %collective-permute-done.3), channel_id=1, source_target_pairs={{0,28},{4,0},{8,4},{12,8},{16,12},{20,16},{24,20},{28,24},{1,29},{... | collective-permute-start | bytes 1572872 | tf_op jit(solution)/shard_map/ppermute | solution.py:20
  105.9 15.7 %collective-permute-start.6 = (bf16[512,512]{1,0:T(8,128)(2,1)}, bf16[512,512]{1,0:T(8,128)(2,1)S(1)}, u32[]{:S(2)}, u32[]{:S(2)}) collective-permute-start(bf16[512,512]{1,0:T(8,128)(2,1)} %collective-permute-done.4), channel_id=1, source_target_pairs={{0,4},{4,8},{8,12},{12,16},{16,20},{20,24},{24,28},{28,0},{1,5},{5... | collective-permute-start | bytes 1572872 | tf_op jit(solution)/shard_map/ppermute | solution.py:17
  123.6 15.8 %all-to-all-start = ((bf16[8,64,128]{2,1,0:T(8,128)(2,1)}), bf16[8,64,128]{2,1,0:T(8,128)(2,1)S(1)}, u32[]{:S(2)}, u32[]{:S(2)}) async-start(bf16[8,64,128]{2,1,0:T(8,128)(2,1)} %bitcast.1), calls=%async_computation | async-start | bytes 262144 | tf_op jit(solution)/shard_map/all_to_all | solution.py:110
  144.6 75.0 %all-to-all-start.2 = ((bf16[8,64,128]{2,1,0:T(8,128)(2,1)}), bf16[8,64,128]{2,1,0:T(8,128)(2,1)S(1)}, u32[]{:S(2)}, u32[]{:S(2)}) async-start(bf16[8,64,128]{2,1,0:T(8,128)(2,1)} %bitcast.11), calls=%async_computation.2 | async-start | bytes 262144 | tf_op jit(solution)/shard_map/all_to_all | solution.py:112
  219.6 11.8 %all-to-all-start.1 = ((bf16[8,64,128]{2,1,0:T(8,128)(2,1)}), bf16[8,64,128]{2,1,0:T(8,128)(2,1)S(1)}, u32[]{:S(2)}, u32[]{:S(2)}) async-start(bf16[8,64,128]{2,1,0:T(8,128)(2,1)} %bitcast.6), calls=%async_computation.1 | async-start | bytes 262144 | tf_op jit(solution)/shard_map/all_to_all | solution.py:111
Sparse Core Ops, SparseCore 0:
  9.5 130.8 all-gather.5
  142.6 72.8 all-gather.3
  217.6 73.2 all-gather.7
